TPU v7x, 256 devices: a whole 4x4x8 slice. The times are simulated.
256 devices in a mesh: layer: 64 (over y, z, core), blk: 4 (over x).
Axes of the slice: x: 4, y: 4, z: 8, core: 2. Of those that a mesh axis runs over, the one named last changes fastest.
Arguments:
- mode_matrix: bfloat16 [128, 512, 512], P(None, 'layer', 'blk'), may hold values from -1 to 1, as said below
- decay_rate: bfloat16 [128, 512], P(None, 'layer'), may hold values from 0.0009994507 to 0.29882812
- facet_refl: bfloat16 [128, 512], P(None, 'layer'), may hold values from -0.796875 to 0.796875
Outputs:
- prefix: bfloat16 [64, 4, 512, 512], P('layer', None, 'blk')
Inputs may be any that keep to these rules, and one draw needn't show every extreme that they name: `mode_matrix`: each layer's matrix has orthonormal columns up to the rounding to bfloat16.
All inputs are finite; a program needn't handle non-finite values.
Results may differ from a plain program's by a relative error of at most 0.0045.
The roundings to bfloat16 on the way count: a program that leaves them out, or rounds other values in their place, can miss the bound.
Values may be sent and summed in bfloat16 or wider, within the bound.
No kernel may reach another device: no remote copies, remote signals or barrier semaphores. Data moves between devices by JAX's collectives and lax.ppermute only.
A program may use at most 64 MiB of HBM per device.

v0:
```python
import jax
import jax.numpy as jnp
from jax import lax
from jax.sharding import PartitionSpec as P

HARM = 512
REFL = 4


def passed_along(value, axis, steps):
    count = lax.axis_size(axis)
    first, last = (max(0, -steps), min(count, count - steps))
    return lax.ppermute(value, axis, [(source, source + steps) for source in range(first, last)])


def times_f32(left_op, right_op):
    return jnp.dot(left_op, right_op, preferred_element_type=jnp.float32)


def star_rows(upper_near, upper_far, lower_near, lower_rows):
    coupling_down = times_f32(lower_near[0], upper_far[1]).astype(jnp.bfloat16)
    coupling_up = times_f32(upper_far[1], lower_near[0]).astype(jnp.bfloat16)
    left_sum = upper_near[1]
    for repeat in range(REFL):
        left_sum = (upper_near[1] + times_f32(left_sum, coupling_down)).astype(jnp.bfloat16)
    right_sum = lower_rows[0]
    for repeat in range(REFL):
        right_sum = (lower_rows[0] + times_f32(right_sum, coupling_up)).astype(jnp.bfloat16)
    left_mid = times_f32(left_sum, lower_near[0]).astype(jnp.bfloat16)
    right_mid = times_f32(right_sum, upper_far[1]).astype(jnp.bfloat16)
    new_refl = (upper_near[0] + times_f32(left_mid, upper_far[0])).astype(jnp.bfloat16)
    new_back = times_f32(left_sum, lower_near[1]).astype(jnp.bfloat16)
    new_fore = times_f32(right_sum, upper_far[0]).astype(jnp.bfloat16)
    new_under = (lower_rows[1] + times_f32(right_mid, lower_near[1])).astype(jnp.bfloat16)
    return jnp.stack([new_refl, new_back, new_fore, new_under])


def on_device(mode_matrix, decay_rate, facet_refl):
    relayed_modes, relayed_decay, relayed_refl = (
        lax.all_to_all(mode_matrix, "layer", split_axis=0, concat_axis=1, tiled=True),
        lax.all_to_all(decay_rate, "layer", split_axis=0, concat_axis=1, tiled=True),
        lax.all_to_all(facet_refl, "layer", split_axis=0, concat_axis=1, tiled=True),
    )
    block_index = lax.axis_index("blk")
    row_count = HARM // lax.axis_size("blk")
    row_start = block_index * row_count
    refl_full = relayed_refl.astype(jnp.float32)
    transmit = jnp.sqrt(1.0 - refl_full * refl_full) * jnp.exp(-relayed_decay.astype(jnp.float32))
    mode_piece = lax.all_gather(relayed_modes, "blk", axis=2, tiled=True)
    piece_wide = mode_piece.astype(jnp.float32)
    scaled_refl = (piece_wide * refl_full[:, None, :]).astype(jnp.bfloat16)
    scaled_tran = (piece_wide * transmit[:, None, :]).astype(jnp.bfloat16)
    own_rows = lax.dynamic_slice_in_dim(mode_piece, row_start, row_count, 1)
    refl_part = jnp.einsum(
        "lhm,lkm->lhk", own_rows, scaled_refl, preferred_element_type=jnp.float32
    )
    tran_part = jnp.einsum(
        "lhm,lkm->lhk", own_rows, scaled_tran, preferred_element_type=jnp.float32
    )
    refl_rows = refl_part.astype(jnp.bfloat16)
    tran_rows = tran_part.astype(jnp.bfloat16)
    layer_rows = jnp.stack([refl_rows, tran_rows, tran_rows, -refl_rows], axis=1)
    layer_pair = lax.all_gather(
        jnp.stack([refl_rows, tran_rows], axis=1), "blk", axis=2, tiled=True
    )
    rows_now = layer_rows[0]
    full_now = jnp.stack([layer_pair[0, 0], layer_pair[0, 1], layer_pair[0, 1], -layer_pair[0, 0]])
    rows_now = star_rows(rows_now[0:2], full_now[2:4], layer_pair[1], layer_rows[1, 2:4])
    full_now = lax.all_gather(rows_now, "blk", axis=1, tiled=True)
    group_index = lax.axis_index("layer")
    level_count = lax.axis_size("layer").bit_length() - 1
    for section_level in range(level_count):
        distance = 1 << section_level
        upper_whole = passed_along(full_now, "layer", distance)
        upper_near = lax.dynamic_slice_in_dim(upper_whole[0:2], row_start, row_count, 1)
        upper_far = upper_whole[2:4]
        combined = star_rows(upper_near, upper_far, full_now[0:2], rows_now[2:4])
        rows_now = jnp.where(group_index >= distance, combined, rows_now)
        if section_level + 1 < level_count:
            full_now = lax.all_gather(rows_now, "blk", axis=1, tiled=True)
    return rows_now[None]


def solution(mesh):
    placed = (P(None, "layer", "blk"), P(None, "layer"), P(None, "layer"))
    return jax.shard_map(
        on_device,
        mesh=mesh,
        in_specs=placed,
        out_specs=P("layer", None, "blk", None),
        check_vma=False,
    )
```

profile of v0, /device:TPU:16, one launch (start us, length us, event | category | flops | bytes accessed | tf_op | source)
XLA Modules:
  0.0 783.8 jit_solution(11975169473791905162)
XLA Ops:
  6.5 23.6 %all_to_all.44 = bf16[128,8,128]{2,1,0:T(8,128)(2,1)S(1)} all-to-all(bf16[128,8,128]{2,1,0:T(8,128)(2,1)} %param.3), channel_id=1, replica_groups=mesh['layer'=64,'blk'=4] {'layer'}, dimensions={0} | all-to-all | bytes 524288 | tf_op jit(solution)/shard_map/all_to_all | solution.py:40
  32.3 6.5 all-to-all-start.1
  40.2 6.3 all-to-all-done.1
  46.5 6.4 all-to-all-start.2
  53.1 7.5 all-to-all-done.2
  65.5 30.2 %all-gather.11.cloned.1.call-done = bf16[2,2,512,512]{3,2,0,1:T(8,128)(2,1)} async-done(((bf16[2,2,128,512]{3,2,0,1:T(8,128)(2,1)}), bf16[2,2,512,512]{3,2,0,1:T(8,128)(2,1)}) %all-gather.11.cloned.1.call-update) | async-done | bytes 2097168 | tf_op jit(solution)/shard_map/all_gather | solution.py:63
  101.8 33.5 %all-gather.13.cloned.1.call-done = bf16[4,512,512]{2,1,0:T(8,128)(2,1)} async-done(((bf16[4,128,512]{2,1,0:T(8,128)(2,1)}), bf16[4,512,512]{2,1,0:T(8,128)(2,1)}) %all-gather.13.cloned.1.call-update) | async-done | bytes 2097168 | tf_op jit(solution)/shard_map/all_gather | solution.py:69
  137.3 27.7 %collective-permute-done = bf16[4,512,512]{2,1,0:T(8,128)(2,1)S(1)} collective-permute-done((bf16[4,512,512]{2,1,0:T(8,128)(2,1)}, bf16[4,512,512]{2,1,0:T(8,128)(2,1)S(1)}, u32[]{:S(2)}, u32[]{:S(2)}) %collective-permute-start) | collective-permute-done | bytes 2097184 | tf_op jit(solution)/shard_map/ppermute | solution.py:13
  178.0 32.6 %all-gather.15.cloned.1.call-done = bf16[4,512,512]{2,1,0:T(8,128)(2,1)} async-done(((bf16[4,128,512]{2,1,0:T(8,128)(2,1)}), bf16[4,512,512]{2,1,0:T(8,128)(2,1)}) %all-gather.15.cloned.1.call-update) | async-done | bytes 2097168 | tf_op jit(solution)/shard_map/all_gather | solution.py:80
  210.7 3.5 collective-permute-start.1
  214.1 48.2 %collective-permute-done.1 = bf16[4,512,512]{2,1,0:T(8,128)(2,1)} collective-permute-done((bf16[4,512,512]{2,1,0:T(8,128)(2,1)}, bf16[4,512,512]{2,1,0:T(8,128)(2,1)}, u32[]{:S(2)}, u32[]{:S(2)}) %collective-permute-start.1) | collective-permute-done | bytes 2097184 | tf_op jit(solution)/shard_map/ppermute | solution.py:13
  275.4 32.6 %all-gather.17.cloned.1.call-done = bf16[4,512,512]{2,1,0:T(8,128)(2,1)} async-done(((bf16[4,128,512]{2,1,0:T(8,128)(2,1)}), bf16[4,512,512]{2,1,0:T(8,128)(2,1)}) %all-gather.17.cloned.1.call-update) | async-done | bytes 2097168 | tf_op jit(solution)/shard_map/all_gather | solution.py:80
  308.1 4.6 collective-permute-start.2
  312.7 93.8 %collective-permute-done.2 = bf16[4,512,512]{2,1,0:T(8,128)(2,1)} collective-permute-done((bf16[4,512,512]{2,1,0:T(8,128)(2,1)}, bf16[4,512,512]{2,1,0:T(8,128)(2,1)}, u32[]{:S(2)}, u32[]{:S(2)}) %collective-permute-start.2) | collective-permute-done | bytes 2097184 | tf_op jit(solution)/shard_map/ppermute | solution.py:13
  421.0 32.6 %all-gather.19.cloned.1.call-done = bf16[4,512,512]{2,1,0:T(8,128)(2,1)} async-done(((bf16[4,128,512]{2,1,0:T(8,128)(2,1)}), bf16[4,512,512]{2,1,0:T(8,128)(2,1)}) %all-gather.19.cloned.1.call-update) | async-done | bytes 2097168 | tf_op jit(solution)/shard_map/all_gather | solution.py:80
  453.6 7.6 collective-permute-start.3
  461.3 80.8 %collective-permute-done.3 = bf16[4,512,512]{2,1,0:T(8,128)(2,1)} collective-permute-done((bf16[4,512,512]{2,1,0:T(8,128)(2,1)}, bf16[4,512,512]{2,1,0:T(8,128)(2,1)}, u32[]{:S(2)}, u32[]{:S(2)}) %collective-permute-start.3) | collective-permute-done | bytes 2097184 | tf_op jit(solution)/shard_map/ppermute | solution.py:13
  559.2 44.1 %all-gather.21.cloned.1.call-done = bf16[4,512,512]{2,1,0:T(8,128)(2,1)} async-done(((bf16[4,128,512]{2,1,0:T(8,128)(2,1)}), bf16[4,512,512]{2,1,0:T(8,128)(2,1)}) %all-gather.21.cloned.1.call-update) | async-done | bytes 2097168 | tf_op jit(solution)/shard_map/all_gather | solution.py:80
  603.4 3.1 collective-permute-start.4
  606.5 46.5 %collective-permute-done.4 = bf16[4,512,512]{2,1,0:T(8,128)(2,1)} collective-permute-done((bf16[4,512,512]{2,1,0:T(8,128)(2,1)}, bf16[4,512,512]{2,1,0:T(8,128)(2,1)}, u32[]{:S(2)}, u32[]{:S(2)}) %collective-permute-start.4) | collective-permute-done | bytes 2097184 | tf_op jit(solution)/shard_map/ppermute | solution.py:13
  662.0 2.4 fusion.32
  672.9 33.6 %all-gather.23.cloned.1.call-done = bf16[4,512,512]{2,1,0:T(8,128)(2,1)} async-done(((bf16[4,128,512]{2,1,0:T(8,128)(2,1)}), bf16[4,512,512]{2,1,0:T(8,128)(2,1)}) %all-gather.23.cloned.1.call-update) | async-done | bytes 2097168 | tf_op jit(solution)/shard_map/all_gather | solution.py:80
  707.7 49.8 %collective-permute-done.5 = bf16[4,512,512]{2,1,0:T(8,128)(2,1)} collective-permute-done((bf16[4,512,512]{2,1,0:T(8,128)(2,1)}, bf16[4,512,512]{2,1,0:T(8,128)(2,1)}, u32[]{:S(2)}, u32[]{:S(2)}) %collective-permute-start.5) | collective-permute-done | bytes 2097184 | tf_op jit(solution)/shard_map/ppermute | solution.py:13
  766.6 2.4 fusion.68
  (160 shorter events, 109.6 us)
Async XLA Ops:
  6.5 54.4 %all-gather.9.cloned.1.call-start = ((), (), s32[]{:S(2)}) async-start(), calls=%async_computation.3 | async-start | bytes 1310720 | tf_op jit(solution)/shard_map/all_gather | solution.py:49
  32.3 14.2 %all-to-all-start.1 = ((bf16[64,2,8]{2,1,0:T(2,128)(2,1)}), bf16[64,2,8]{2,1,0:T(2,128)(2,1)S(1)}, u32[]{:S(2)}, u32[]{:S(2)}) async-start(bf16[64,2,8]{2,1,0:T(2,128)(2,1)} %bitcast.3), calls=%async_computation.1 | async-start | bytes 65536 | tf_op jit(solution)/shard_map/all_to_all | solution.py:42
  46.5 14.1 %all-to-all-start.2 = ((bf16[64,2,8]{2,1,0:T(2,128)(2,1)}), bf16[64,2,8]{2,1,0:T(2,128)(2,1)S(1)}, u32[]{:S(2)}, u32[]{:S(2)}) async-start(bf16[64,2,8]{2,1,0:T(2,128)(2,1)} %bitcast.6), calls=%async_computation.2 | async-start | bytes 65536 | tf_op jit(solution)/shard_map/all_to_all | solution.py:41
  52.9 42.8 %all-gather.11.cloned.1.call-start = ((), (), s32[]{:S(2)}) async-start(), calls=%async_computation.4 | async-start | bytes 2621440 | tf_op jit(solution)/shard_map/all_gather | solution.py:63
  65.4 69.9 %all-gather.13.cloned.1.call-start = ((), (), s32[]{:S(2)}) async-start(), calls=%async_computation.5 | async-start | bytes 2621440 | tf_op jit(solution)/shard_map/all_gather | solution.py:69
  101.7 108.9 %all-gather.15.cloned.1.call-start = ((), (), s32[]{:S(2)}) async-start(), calls=%async_computation.6 | async-start | bytes 2621440 | tf_op jit(solution)/shard_map/all_gather | solution.py:80
  135.3 29.7 %collective-permute-start = (bf16[4,512,512]{2,1,0:T(8,128)(2,1)}, bf16[4,512,512]{2,1,0:T(8,128)(2,1)S(1)}, u32[]{:S(2)}, u32[]{:S(2)}) collective-permute-start(bf16[4,512,512]{2,1,0:T(8,128)(2,1)} %all-gather.13.cloned.1.call-done), channel_id=1, source_target_pairs={{0,4},{4,8},{8,12},{12,16},{16,20},{20,24},{24,28},{28,32},{32,36}... | collective-permute-start | bytes 6291464 | tf_op jit(solution)/shard_map/ppermute | solution.py:13
  178.0 86.0 %copy-start.1 = (bf16[4,128,512]{2,1,0:T(8,128)(2,1)S(1)}, bf16[4,128,512]{2,1,0:T(8,128)(2,1)}, u32[]{:S(2)}) copy-start(bf16[4,128,512]{2,1,0:T(8,128)(2,1)} %maximum_select_fusion) | copy-start | bytes 1572868
  178.0 130.1 %all-gather.17.cloned.1.call-start = ((), (), s32[]{:S(2)}) async-start(), calls=%async_computation.7 | async-start | bytes 2621440 | tf_op jit(solution)/shard_map/all_gather | solution.py:80
  210.7 51.7 %collective-permute-start.1 = (bf16[4,512,512]{2,1,0:T(8,128)(2,1)}, bf16[4,512,512]{2,1,0:T(8,128)(2,1)}, u32[]{:S(2)}, u32[]{:S(2)}) collective-permute-start(bf16[4,512,512]{2,1,0:T(8,128)(2,1)} %all-gather.15.cloned.1.call-done), channel_id=1, source_target_pairs={{0,8},{4,12},{8,16},{12,20},{16,24},{20,28},{24,32},{28,36},{32,40... | collective-permute-start | bytes 6291464 | tf_op jit(solution)/shard_map/ppermute | solution.py:13
  275.4 132.7 %copy-start.2 = (bf16[4,128,512]{2,1,0:T(8,128)(2,1)S(1)}, bf16[4,128,512]{2,1,0:T(8,128)(2,1)}, u32[]{:S(2)}) copy-start(bf16[4,128,512]{2,1,0:T(8,128)(2,1)} %maximum_select_fusion.1) | copy-start | bytes 1572868
  275.4 178.2 %all-gather.19.cloned.1.call-start = ((), (), s32[]{:S(2)}) async-start(), calls=%async_computation.8 | async-start | bytes 2621440 | tf_op jit(solution)/shard_map/all_gather | solution.py:80
  308.1 98.4 %collective-permute-start.2 = (bf16[4,512,512]{2,1,0:T(8,128)(2,1)}, bf16[4,512,512]{2,1,0:T(8,128)(2,1)}, u32[]{:S(2)}, u32[]{:S(2)}) collective-permute-start(bf16[4,512,512]{2,1,0:T(8,128)(2,1)} %all-gather.17.cloned.1.call-done), channel_id=1, source_target_pairs={{0,16},{4,20},{8,24},{12,28},{16,32},{20,36},{24,40},{28,44},{32,4... | collective-permute-start | bytes 6291464 | tf_op jit(solution)/shard_map/ppermute | solution.py:13
  420.9 122.8 %copy-start.3 = (bf16[4,128,512]{2,1,0:T(8,128)(2,1)S(1)}, bf16[4,128,512]{2,1,0:T(8,128)(2,1)}, u32[]{:S(2)}) copy-start(bf16[4,128,512]{2,1,0:T(8,128)(2,1)} %maximum_select_fusion.2) | copy-start | bytes 1572868
  420.9 182.4 %all-gather.21.cloned.1.call-start = ((), (), s32[]{:S(2)}) async-start(), calls=%async_computation.9 | async-start | bytes 2621440 | tf_op jit(solution)/shard_map/all_gather | solution.py:80
  453.6 88.5 %collective-permute-start.3 = (bf16[4,512,512]{2,1,0:T(8,128)(2,1)}, bf16[4,512,512]{2,1,0:T(8,128)(2,1)}, u32[]{:S(2)}, u32[]{:S(2)}) collective-permute-start(bf16[4,512,512]{2,1,0:T(8,128)(2,1)} %all-gather.19.cloned.1.call-done), channel_id=1, source_target_pairs={{0,32},{4,36},{8,40},{12,44},{16,48},{20,52},{24,56},{28,60},{32,6... | collective-permute-start | bytes 6291464 | tf_op jit(solution)/shard_map/ppermute | solution.py:13
  559.1 95.4 %copy-start.4 = (bf16[4,128,512]{2,1,0:T(8,128)(2,1)S(1)}, bf16[4,128,512]{2,1,0:T(8,128)(2,1)}, u32[]{:S(2)}) copy-start(bf16[4,128,512]{2,1,0:T(8,128)(2,1)} %maximum_select_fusion.3) | copy-start | bytes 1572868
  559.2 147.3 %all-gather.23.cloned.1.call-start = ((), (), s32[]{:S(2)}) async-start(), calls=%async_computation.10 | async-start | bytes 2621440 | tf_op jit(solution)/shard_map/all_gather | solution.py:80
  603.4 49.6 %collective-permute-start.4 = (bf16[4,512,512]{2,1,0:T(8,128)(2,1)}, bf16[4,512,512]{2,1,0:T(8,128)(2,1)}, u32[]{:S(2)}, u32[]{:S(2)}) collective-permute-start(bf16[4,512,512]{2,1,0:T(8,128)(2,1)} %all-gather.21.cloned.1.call-done), channel_id=1, source_target_pairs={{0,64},{4,68},{8,72},{12,76},{16,80},{20,84},{24,88},{28,92},{32,9... | collective-permute-start | bytes 6291464 | tf_op jit(solution)/shard_map/ppermute | solution.py:13
  662.0 8.7 %copy-start.10 = (bf16[128,512]{1,0:T(8,128)(2,1)S(1)}, bf16[128,512]{1,0:T(8,128)(2,1)}, u32[]{:S(2)}) copy-start(bf16[128,512]{1,0:T(8,128)(2,1)} %copy-done.9) | copy-start | bytes 393220
  662.0 8.7 %copy-start.13 = (bf16[128,512]{1,0:T(8,128)(2,1)S(1)}, bf16[128,512]{1,0:T(8,128)(2,1)}, u32[]{:S(2)}) copy-start(bf16[128,512]{1,0:T(8,128)(2,1)} %copy-done.12) | copy-start | bytes 393220
  662.0 8.7 %copy-start.16 = (bf16[128,512]{1,0:T(8,128)(2,1)S(1)}, bf16[128,512]{1,0:T(8,128)(2,1)}, u32[]{:S(2)}) copy-start(bf16[128,512]{1,0:T(8,128)(2,1)} %copy-done.15) | copy-start | bytes 393220
  672.8 86.3 %copy-start = (bf16[4,128,512]{2,1,0:T(8,128)(2,1)S(1)}, bf16[4,128,512]{2,1,0:T(8,128)(2,1)}, u32[]{:S(2)}) copy-start(bf16[4,128,512]{2,1,0:T(8,128)(2,1)} %maximum_select_fusion.4) | copy-start | bytes 1572868
  706.4 51.1 %collective-permute-start.5 = (bf16[4,512,512]{2,1,0:T(8,128)(2,1)}, bf16[4,512,512]{2,1,0:T(8,128)(2,1)}, u32[]{:S(2)}, u32[]{:S(2)}) collective-permute-start(bf16[4,512,512]{2,1,0:T(8,128)(2,1)} %all-gather.23.cloned.1.call-done), channel_id=1, source_target_pairs={{0,128},{4,132},{8,136},{12,140},{16,144},{20,148},{24,152},{28,15... | collective-permute-start | bytes 6291464 | tf_op jit(solution)/shard_map/ppermute | solution.py:13
  (15 other events, 72.3 us)
Sparse Core Ops, SparseCore 0:
  31.0 25.5 all-gather.8
  65.5 30.0 all-gather.10
  101.9 33.4 all-gather.12
  178.1 32.5 all-gather.14
  275.5 32.5 all-gather.16
  421.0 32.5 all-gather.18
  559.3 44.0 all-gather.20
  673.0 33.4 all-gather.22
where the time goes:
time: 786 us; the launch traced here: 784 us
  waiting for transfers between devices  600 us (76%)
  matrix products  86.9 us (11%)
  starting transfers between devices  35.1 us (4%)
  blocking collectives  23.6 us (3%)
  between operations  14.3 us (2%)
  local copies, waits for them, and re-layouts  13.7 us (2%)
  other arithmetic  10.2 us (1%)
    ppermute x6, waiting for transfers between devices, passed_along(): lax.ppermute(value, axis, [(source, source + steps) for source in range(f...  347 us
    all_gather x6, waiting for transfers between devices, on_device(): full_now = lax.all_gather(rows_now, 'blk', axis=1, tiled=True)  209 us
    dot_general x70, matrix products, times_f32(): return jnp.dot(left_op, right_op, preferred_element_type=jnp.float32)  83.3 us
    all_gather x1, waiting for transfers between devices, on_device(): lax.all_gather(jnp.stack([refl_rows, tran_rows], axis=1), 'blk', axis=2,...  30.2 us
    all_to_all x1, blocking collectives, on_device(): lax.all_to_all(mode_matrix, 'layer', split_axis=0, concat_axis=1, tiled=T...  23.6 us
    ppermute x6, starting transfers between devices, passed_along(): lax.ppermute(value, axis, [(source, source + steps) for source in range(f...  22 us
  transfers between devices with their start and end apart: 16, of which 15 were waited for; matrix products, arithmetic and copies ran while one was open for 0% of the time, Pallas kernels for 0%

commit v1 on v0

--- a/solution.py
+++ b/solution.py
@@ -37,7 +37,12 @@
 
 def on_device(mode_matrix, decay_rate, facet_refl):
     relayed_modes, relayed_decay, relayed_refl = (
-        lax.all_to_all(mode_matrix, "layer", split_axis=0, concat_axis=1, tiled=True),
+        jnp.concatenate(
+            lax.all_to_all(
+                jnp.stack(jnp.split(mode_matrix, lax.axis_size("layer"), axis=0)), "layer", 0, 0
+            ),
+            axis=1,
+        ),
         lax.all_to_all(decay_rate, "layer", split_axis=0, concat_axis=1, tiled=True),
         lax.all_to_all(facet_refl, "layer", split_axis=0, concat_axis=1, tiled=True),
     )

time: 786 us -> 832 us (1.059)
  local copies, waits for them, and re-layouts: 13.7 us -> 58 us
    unnamed x48 -> x111, local copies, waits for them, and re-layouts: 4.82 us -> 48.5 us
where the time goes in v1:
time: 832 us; the launch traced here: 828 us
  waiting for transfers between devices  600 us (72%)
  matrix products  87 us (10%)
  local copies, waits for them, and re-layouts  58 us (7%)
  starting transfers between devices  35.1 us (4%)
  blocking collectives  23.4 us (3%)
  between operations  14.3 us (2%)
  other arithmetic  10.2 us (1%)
    ppermute x6, waiting for transfers between devices, passed_along(): lax.ppermute(value, axis, [(source, source + steps) for source in range(f...  347 us
    all_gather x6, waiting for transfers between devices, on_device(): full_now = lax.all_gather(rows_now, 'blk', axis=1, tiled=True)  209 us
    dot_general x70, matrix products, times_f32(): return jnp.dot(left_op, right_op, preferred_element_type=jnp.float32)  83.4 us
    unnamed x111, local copies, waits for them, and re-layouts  48.5 us
    all_gather x1, waiting for transfers between devices, on_device(): lax.all_gather(jnp.stack([refl_rows, tran_rows], axis=1), 'blk', axis=2,...  30.2 us
    all_to_all x1, blocking collectives, on_device(): lax.all_to_all(jnp.stack(jnp.split(mode_matrix, lax.axis_size('layer'), a...  23.4 us
    ppermute x6, starting transfers between devices, passed_along(): lax.ppermute(value, axis, [(source, source + steps) for source in range(f...  22 us
  transfers between devices with their start and end apart: 16, of which 15 were waited for; matrix products, arithmetic and copies ran while one was open for 0% of the time, Pallas kernels for 0%

profile of v1, /device:TPU:16, one launch (start us, length us, event | category | flops | bytes accessed | tf_op | source)
XLA Modules:
  0.0 828.2 jit_solution(918376820625078141)
XLA Ops:
  50.9 23.4 %all_to_all.31 = bf16[64,2,8,128]{3,2,1,0:T(8,128)(2,1)S(1)} all-to-all(bf16[64,2,8,128]{3,2,1,0:T(8,128)(2,1)S(1)} %constant_dynamic-update-slice_fusion), channel_id=1, replica_groups=mesh['layer'=64,'blk'=4] {'layer'}, dimensions={0} | all-to-all | bytes 524288 | tf_op jit(solution)/shard_map/all_to_all | solution.py:41
  76.5 6.5 all-to-all-start.1
  84.4 6.3 all-to-all-done.1
  90.7 6.4 all-to-all-start.2
  97.3 7.5 all-to-all-done.2
  109.7 30.2 %all-gather.11.cloned.1.call-done = bf16[2,2,512,512]{3,2,0,1:T(8,128)(2,1)} async-done(((bf16[2,2,128,512]{3,2,0,1:T(8,128)(2,1)}), bf16[2,2,512,512]{3,2,0,1:T(8,128)(2,1)}) %all-gather.11.cloned.1.call-update) | async-done | bytes 2097168 | tf_op jit(solution)/shard_map/all_gather | solution.py:68
  146.0 33.5 %all-gather.13.cloned.1.call-done = bf16[4,512,512]{2,1,0:T(8,128)(2,1)} async-done(((bf16[4,128,512]{2,1,0:T(8,128)(2,1)}), bf16[4,512,512]{2,1,0:T(8,128)(2,1)}) %all-gather.13.cloned.1.call-update) | async-done | bytes 2097168 | tf_op jit(solution)/shard_map/all_gather | solution.py:74
  181.4 27.7 %collective-permute-done = bf16[4,512,512]{2,1,0:T(8,128)(2,1)S(1)} collective-permute-done((bf16[4,512,512]{2,1,0:T(8,128)(2,1)}, bf16[4,512,512]{2,1,0:T(8,128)(2,1)S(1)}, u32[]{:S(2)}, u32[]{:S(2)}) %collective-permute-start) | collective-permute-done | bytes 2097184 | tf_op jit(solution)/shard_map/ppermute | solution.py:13
  222.4 32.6 %all-gather.15.cloned.1.call-done = bf16[4,512,512]{2,1,0:T(8,128)(2,1)} async-done(((bf16[4,128,512]{2,1,0:T(8,128)(2,1)}), bf16[4,512,512]{2,1,0:T(8,128)(2,1)}) %all-gather.15.cloned.1.call-update) | async-done | bytes 2097168 | tf_op jit(solution)/shard_map/all_gather | solution.py:85
  255.0 3.5 collective-permute-start.1
  258.5 48.2 %collective-permute-done.1 = bf16[4,512,512]{2,1,0:T(8,128)(2,1)} collective-permute-done((bf16[4,512,512]{2,1,0:T(8,128)(2,1)}, bf16[4,512,512]{2,1,0:T(8,128)(2,1)}, u32[]{:S(2)}, u32[]{:S(2)}) %collective-permute-start.1) | collective-permute-done | bytes 2097184 | tf_op jit(solution)/shard_map/ppermute | solution.py:13
  319.8 32.6 %all-gather.17.cloned.1.call-done = bf16[4,512,512]{2,1,0:T(8,128)(2,1)} async-done(((bf16[4,128,512]{2,1,0:T(8,128)(2,1)}), bf16[4,512,512]{2,1,0:T(8,128)(2,1)}) %all-gather.17.cloned.1.call-update) | async-done | bytes 2097168 | tf_op jit(solution)/shard_map/all_gather | solution.py:85
  352.4 4.6 collective-permute-start.2
  357.0 93.8 %collective-permute-done.2 = bf16[4,512,512]{2,1,0:T(8,128)(2,1)} collective-permute-done((bf16[4,512,512]{2,1,0:T(8,128)(2,1)}, bf16[4,512,512]{2,1,0:T(8,128)(2,1)}, u32[]{:S(2)}, u32[]{:S(2)}) %collective-permute-start.2) | collective-permute-done | bytes 2097184 | tf_op jit(solution)/shard_map/ppermute | solution.py:13
  465.3 32.6 %all-gather.19.cloned.1.call-done = bf16[4,512,512]{2,1,0:T(8,128)(2,1)} async-done(((bf16[4,128,512]{2,1,0:T(8,128)(2,1)}), bf16[4,512,512]{2,1,0:T(8,128)(2,1)}) %all-gather.19.cloned.1.call-update) | async-done | bytes 2097168 | tf_op jit(solution)/shard_map/all_gather | solution.py:85
  497.9 7.6 collective-permute-start.3
  505.6 80.8 %collective-permute-done.3 = bf16[4,512,512]{2,1,0:T(8,128)(2,1)} collective-permute-done((bf16[4,512,512]{2,1,0:T(8,128)(2,1)}, bf16[4,512,512]{2,1,0:T(8,128)(2,1)}, u32[]{:S(2)}, u32[]{:S(2)}) %collective-permute-start.3) | collective-permute-done | bytes 2097184 | tf_op jit(solution)/shard_map/ppermute | solution.py:13
  603.6 44.1 %all-gather.21.cloned.1.call-done = bf16[4,512,512]{2,1,0:T(8,128)(2,1)} async-done(((bf16[4,128,512]{2,1,0:T(8,128)(2,1)}), bf16[4,512,512]{2,1,0:T(8,128)(2,1)}) %all-gather.21.cloned.1.call-update) | async-done | bytes 2097168 | tf_op jit(solution)/shard_map/all_gather | solution.py:85
  647.7 3.1 collective-permute-start.4
  650.8 46.5 %collective-permute-done.4 = bf16[4,512,512]{2,1,0:T(8,128)(2,1)} collective-permute-done((bf16[4,512,512]{2,1,0:T(8,128)(2,1)}, bf16[4,512,512]{2,1,0:T(8,128)(2,1)}, u32[]{:S(2)}, u32[]{:S(2)}) %collective-permute-start.4) | collective-permute-done | bytes 2097184 | tf_op jit(solution)/shard_map/ppermute | solution.py:13
  706.4 2.4 fusion.32
  717.2 33.6 %all-gather.23.cloned.1.call-done = bf16[4,512,512]{2,1,0:T(8,128)(2,1)} async-done(((bf16[4,128,512]{2,1,0:T(8,128)(2,1)}), bf16[4,512,512]{2,1,0:T(8,128)(2,1)}) %all-gather.23.cloned.1.call-update) | async-done | bytes 2097168 | tf_op jit(solution)/shard_map/all_gather | solution.py:85
  752.1 49.8 %collective-permute-done.5 = bf16[4,512,512]{2,1,0:T(8,128)(2,1)} collective-permute-done((bf16[4,512,512]{2,1,0:T(8,128)(2,1)}, bf16[4,512,512]{2,1,0:T(8,128)(2,1)}, u32[]{:S(2)}, u32[]{:S(2)}) %collective-permute-start.5) | collective-permute-done | bytes 2097184 | tf_op jit(solution)/shard_map/ppermute | solution.py:13
  811.0 2.4 fusion.68
  (224 shorter events, 154.1 us)
Async XLA Ops:
  6.5 98.6 %all-gather.9.cloned.1.call-start = ((), (), s32[]{:S(2)}) async-start(), calls=%async_computation.3 | async-start | bytes 1310720 | tf_op jit(solution)/shard_map/all_gather | solution.py:54
  76.5 14.2 %all-to-all-start.1 = ((bf16[64,2,8]{2,1,0:T(2,128)(2,1)}), bf16[64,2,8]{2,1,0:T(2,128)(2,1)S(1)}, u32[]{:S(2)}, u32[]{:S(2)}) async-start(bf16[64,2,8]{2,1,0:T(2,128)(2,1)} %bitcast.66), calls=%async_computation.1 | async-start | bytes 65536 | tf_op jit(solution)/shard_map/all_to_all | solution.py:47
  90.7 14.1 %all-to-all-start.2 = ((bf16[64,2,8]{2,1,0:T(2,128)(2,1)}), bf16[64,2,8]{2,1,0:T(2,128)(2,1)S(1)}, u32[]{:S(2)}, u32[]{:S(2)}) async-start(bf16[64,2,8]{2,1,0:T(2,128)(2,1)} %bitcast.69), calls=%async_computation.2 | async-start | bytes 65536 | tf_op jit(solution)/shard_map/all_to_all | solution.py:46
  97.1 42.8 %all-gather.11.cloned.1.call-start = ((), (), s32[]{:S(2)}) async-start(), calls=%async_computation.4 | async-start | bytes 2621440 | tf_op jit(solution)/shard_map/all_gather | solution.py:68
  109.6 69.9 %all-gather.13.cloned.1.call-start = ((), (), s32[]{:S(2)}) async-start(), calls=%async_computation.5 | async-start | bytes 2621440 | tf_op jit(solution)/shard_map/all_gather | solution.py:74
  145.9 109.1 %all-gather.15.cloned.1.call-start = ((), (), s32[]{:S(2)}) async-start(), calls=%async_computation.6 | async-start | bytes 2621440 | tf_op jit(solution)/shard_map/all_gather | solution.py:85
  179.5 29.7 %collective-permute-start = (bf16[4,512,512]{2,1,0:T(8,128)(2,1)}, bf16[4,512,512]{2,1,0:T(8,128)(2,1)S(1)}, u32[]{:S(2)}, u32[]{:S(2)}) collective-permute-start(bf16[4,512,512]{2,1,0:T(8,128)(2,1)} %all-gather.13.cloned.1.call-done), channel_id=1, source_target_pairs={{0,4},{4,8},{8,12},{12,16},{16,20},{20,24},{24,28},{28,32},{32,36}... | collective-permute-start | bytes 6291464 | tf_op jit(solution)/shard_map/ppermute | solution.py:13
  222.3 86.0 %copy-start.1 = (bf16[4,128,512]{2,1,0:T(8,128)(2,1)S(1)}, bf16[4,128,512]{2,1,0:T(8,128)(2,1)}, u32[]{:S(2)}) copy-start(bf16[4,128,512]{2,1,0:T(8,128)(2,1)} %maximum_select_fusion) | copy-start | bytes 1572868
  222.3 130.1 %all-gather.17.cloned.1.call-start = ((), (), s32[]{:S(2)}) async-start(), calls=%async_computation.7 | async-start | bytes 2621440 | tf_op jit(solution)/shard_map/all_gather | solution.py:85
  255.0 51.7 %collective-permute-start.1 = (bf16[4,512,512]{2,1,0:T(8,128)(2,1)}, bf16[4,512,512]{2,1,0:T(8,128)(2,1)}, u32[]{:S(2)}, u32[]{:S(2)}) collective-permute-start(bf16[4,512,512]{2,1,0:T(8,128)(2,1)} %all-gather.15.cloned.1.call-done), channel_id=1, source_target_pairs={{0,8},{4,12},{8,16},{12,20},{16,24},{20,28},{24,32},{28,36},{32,40... | collective-permute-start | bytes 6291464 | tf_op jit(solution)/shard_map/ppermute | solution.py:13
  319.7 132.7 %copy-start.2 = (bf16[4,128,512]{2,1,0:T(8,128)(2,1)S(1)}, bf16[4,128,512]{2,1,0:T(8,128)(2,1)}, u32[]{:S(2)}) copy-start(bf16[4,128,512]{2,1,0:T(8,128)(2,1)} %maximum_select_fusion.1) | copy-start | bytes 1572868
  319.7 178.2 %all-gather.19.cloned.1.call-start = ((), (), s32[]{:S(2)}) async-start(), calls=%async_computation.8 | async-start | bytes 2621440 | tf_op jit(solution)/shard_map/all_gather | solution.py:85
  352.4 98.4 %collective-permute-start.2 = (bf16[4,512,512]{2,1,0:T(8,128)(2,1)}, bf16[4,512,512]{2,1,0:T(8,128)(2,1)}, u32[]{:S(2)}, u32[]{:S(2)}) collective-permute-start(bf16[4,512,512]{2,1,0:T(8,128)(2,1)} %all-gather.17.cloned.1.call-done), channel_id=1, source_target_pairs={{0,16},{4,20},{8,24},{12,28},{16,32},{20,36},{24,40},{28,44},{32,4... | collective-permute-start | bytes 6291464 | tf_op jit(solution)/shard_map/ppermute | solution.py:13
  465.2 122.8 %copy-start.3 = (bf16[4,128,512]{2,1,0:T(8,128)(2,1)S(1)}, bf16[4,128,512]{2,1,0:T(8,128)(2,1)}, u32[]{:S(2)}) copy-start(bf16[4,128,512]{2,1,0:T(8,128)(2,1)} %maximum_select_fusion.2) | copy-start | bytes 1572868
  465.3 182.4 %all-gather.21.cloned.1.call-start = ((), (), s32[]{:S(2)}) async-start(), calls=%async_computation.9 | async-start | bytes 2621440 | tf_op jit(solution)/shard_map/all_gather | solution.py:85
  497.9 88.5 %collective-permute-start.3 = (bf16[4,512,512]{2,1,0:T(8,128)(2,1)}, bf16[4,512,512]{2,1,0:T(8,128)(2,1)}, u32[]{:S(2)}, u32[]{:S(2)}) collective-permute-start(bf16[4,512,512]{2,1,0:T(8,128)(2,1)} %all-gather.19.cloned.1.call-done), channel_id=1, source_target_pairs={{0,32},{4,36},{8,40},{12,44},{16,48},{20,52},{24,56},{28,60},{32,6... | collective-permute-start | bytes 6291464 | tf_op jit(solution)/shard_map/ppermute | solution.py:13
  603.5 95.4 %copy-start.4 = (bf16[4,128,512]{2,1,0:T(8,128)(2,1)S(1)}, bf16[4,128,512]{2,1,0:T(8,128)(2,1)}, u32[]{:S(2)}) copy-start(bf16[4,128,512]{2,1,0:T(8,128)(2,1)} %maximum_select_fusion.3) | copy-start | bytes 1572868
  603.5 147.3 %all-gather.23.cloned.1.call-start = ((), (), s32[]{:S(2)}) async-start(), calls=%async_computation.10 | async-start | bytes 2621440 | tf_op jit(solution)/shard_map/all_gather | solution.py:85
  647.7 49.6 %collective-permute-start.4 = (bf16[4,512,512]{2,1,0:T(8,128)(2,1)}, bf16[4,512,512]{2,1,0:T(8,128)(2,1)}, u32[]{:S(2)}, u32[]{:S(2)}) collective-permute-start(bf16[4,512,512]{2,1,0:T(8,128)(2,1)} %all-gather.21.cloned.1.call-done), channel_id=1, source_target_pairs={{0,64},{4,68},{8,72},{12,76},{16,80},{20,84},{24,88},{28,92},{32,9... | collective-permute-start | bytes 6291464 | tf_op jit(solution)/shard_map/ppermute | solution.py:13
  706.4 8.7 %copy-start.10 = (bf16[128,512]{1,0:T(8,128)(2,1)S(1)}, bf16[128,512]{1,0:T(8,128)(2,1)}, u32[]{:S(2)}) copy-start(bf16[128,512]{1,0:T(8,128)(2,1)} %copy-done.9) | copy-start | bytes 393220
  706.4 8.7 %copy-start.13 = (bf16[128,512]{1,0:T(8,128)(2,1)S(1)}, bf16[128,512]{1,0:T(8,128)(2,1)}, u32[]{:S(2)}) copy-start(bf16[128,512]{1,0:T(8,128)(2,1)} %copy-done.12) | copy-start | bytes 393220
  706.4 8.7 %copy-start.16 = (bf16[128,512]{1,0:T(8,128)(2,1)S(1)}, bf16[128,512]{1,0:T(8,128)(2,1)}, u32[]{:S(2)}) copy-start(bf16[128,512]{1,0:T(8,128)(2,1)} %copy-done.15) | copy-start | bytes 393220
  717.2 86.3 %copy-start = (bf16[4,128,512]{2,1,0:T(8,128)(2,1)S(1)}, bf16[4,128,512]{2,1,0:T(8,128)(2,1)}, u32[]{:S(2)}) copy-start(bf16[4,128,512]{2,1,0:T(8,128)(2,1)} %maximum_select_fusion.4) | copy-start | bytes 1572868
  750.8 51.1 %collective-permute-start.5 = (bf16[4,512,512]{2,1,0:T(8,128)(2,1)}, bf16[4,512,512]{2,1,0:T(8,128)(2,1)}, u32[]{:S(2)}, u32[]{:S(2)}) collective-permute-start(bf16[4,512,512]{2,1,0:T(8,128)(2,1)} %all-gather.23.cloned.1.call-done), channel_id=1, source_target_pairs={{0,128},{4,132},{8,136},{12,140},{16,144},{20,148},{24,152},{28,15... | collective-permute-start | bytes 6291464 | tf_op jit(solution)/shard_map/ppermute | solution.py:13
  (15 other events, 71.9 us)
Sparse Core Ops, SparseCore 0:
  75.2 25.5 all-gather.8
  109.7 30.0 all-gather.10
  146.0 33.4 all-gather.12
  222.5 32.5 all-gather.14
  319.8 32.5 all-gather.16
  465.4 32.5 all-gather.18
  603.6 44.0 all-gather.20
  717.3 33.4 all-gather.22
